TPU v7x, 32 devices: a whole 2x2x4 slice. The times are simulated.
32 devices in a mesh: groups: 2 (over x), gz: 16 (over z, y, core).
Axes of the slice: x: 2, y: 2, z: 4, core: 2. Of those that a mesh axis runs over, the one named last changes fastest.
Arguments:
- waves: bfloat16 [192, 8, 64, 256], P(('groups', 'gz')), parts along dimension 0, may hold values from -6 to 6
- potential: float32 [192, 512], P(('groups', 'gz')), parts along dimension 0, may hold values from 0.25 to 4
- domain_of: int32 [32], P('groups'), parts along dimension 0, may hold values from 0 to 7, never falling along the last dimension, each value on 1 to 9 neighbouring positions
Outputs:
- orbitals: bfloat16 [192, 8, 64, 256], P(('groups', 'gz')), parts along dimension 0
There are 2 independent parts, one for each index of `groups`. A program takes and returns all parts, laid end to end along the dimension named above; each array names one. Nothing has to cross between parts.
Inputs may be any that keep to these rules, and one draw needn't show every extreme that they name: `domain_of`: never falls; every domain holds 1 to 9 blocks, one domain exactly that many.
All inputs are finite; a program needn't handle non-finite values.
Results may differ from a plain program's by a relative error of at most 0.0038.
The roundings to bfloat16 on the way count: a program that leaves them out, or rounds other values in their place, can miss the bound.
Values may be sent and summed in bfloat16 or wider, within the bound.
No kernel may reach another device: no remote copies, remote signals or barrier semaphores. Data moves between devices by JAX's collectives and lax.ppermute only.
A program may use at most 64 MiB of HBM per device.

v0:
```python
import jax
import jax.numpy as jnp
from jax import lax
from jax.sharding import PartitionSpec as P

PANEL = 128
NX = 64
NY = 8
DOMS = 8
DEGREE = 4
COEF = (-49.0 / 18.0, 1.5, -0.15, 1.0 / 90.0)
CSHIFT = 7.0
EWIDTH = 5.0


def extended_2(block, sides, width):
    for axis, dim in sides:
        count = lax.axis_size(axis)
        forward = [(i, i + 1) for i in range(count - 1)]
        backward = [(target, source) for source, target in forward]
        low = lax.ppermute(
            lax.slice_in_dim(block, block.shape[dim] - width, None, axis=dim), axis, forward
        )
        high = lax.ppermute(lax.slice_in_dim(block, 0, width, axis=dim), axis, backward)
        block = jnp.concatenate([low, block, high], axis=dim)
    return block


def hamiltonian(extended, potential):
    inner = extended[3:-3]
    planes = inner.shape[0]
    rows_y = inner.shape[1]
    rows_x = inner.shape[2]
    padded_y = jnp.pad(inner, ((0, 0), (3, 3), (0, 0), (0, 0)))
    padded_x = jnp.pad(inner, ((0, 0), (0, 0), (3, 3), (0, 0)))
    total = 3.0 * COEF[0] * inner
    for distance in (1, 2, 3):
        along_z = (
            extended[3 + distance : 3 + distance + planes]
            + extended[3 - distance : 3 - distance + planes]
        )
        along_y = (
            padded_y[:, 3 + distance : 3 + distance + rows_y]
            + padded_y[:, 3 - distance : 3 - distance + rows_y]
        )
        along_x = (
            padded_x[:, :, 3 + distance : 3 + distance + rows_x]
            + padded_x[:, :, 3 - distance : 3 - distance + rows_x]
        )
        total = total + COEF[distance] * (along_z + along_y + along_x)
    return potential[:, :, :, None] * inner - 0.5 * total


def shards(waves, potential, domain_of):
    slabs = lax.axis_size("gz")
    position = lax.axis_index("gz")
    planes = waves.shape[0]
    bands = waves.shape[3]
    grid = potential.reshape(planes, NY, NX)
    owner = domain_of[position]
    below = jnp.where(position > 0, domain_of[jnp.maximum(position - 1, 0)] == owner, False).astype(
        jnp.float32
    )
    above = jnp.where(
        position < slabs - 1, domain_of[jnp.minimum(position + 1, slabs - 1)] == owner, False
    ).astype(jnp.float32)
    mask_three = jnp.concatenate(
        [
            jnp.broadcast_to(below, (3,)),
            jnp.ones((planes,), jnp.float32),
            jnp.broadcast_to(above, (3,)),
        ]
    )[:, None, None, None]

    def rimmed(field):
        return extended_2(field, (("gz", 0),), 3).astype(jnp.float32) * mask_three

    extended = rimmed(waves)
    image = hamiltonian(extended, grid)
    older = waves
    current = ((image - CSHIFT * extended[3:-3]) / EWIDTH).astype(jnp.bfloat16)
    for turn in range(DEGREE - 1):
        extended = rimmed(current)
        image = hamiltonian(extended, grid)
        newer = (
            2.0 / EWIDTH * (image - CSHIFT * extended[3:-3]) - older.astype(jnp.float32)
        ).astype(jnp.bfloat16)
        older, current = (current, newer)
    cells = jnp.sum((domain_of == owner).astype(jnp.float32)) * (planes * NY * NX)
    rows = current.reshape(planes * NY * NX, bands)

    def domain_total(term):
        picker = (jnp.arange(DOMS) == owner).astype(jnp.float32)
        summed = lax.psum(picker[:, None, None] * term[None], "gz")
        return jnp.sum(picker[:, None, None] * summed, axis=0)

    identity = jnp.eye(PANEL, dtype=jnp.float32)
    pieces = []
    for panel in range(bands // PANEL):
        block = rows[:, panel * PANEL : (panel + 1) * PANEL]
        if panel > 0:
            earlier = pieces[0]
            correlation = (
                domain_total(
                    jnp.einsum("ca,cb->ab", earlier, block, preferred_element_type=jnp.float32)
                )
                / cells
            )
            block = (
                block.astype(jnp.float32)
                - jnp.dot(
                    earlier, correlation.astype(jnp.bfloat16), preferred_element_type=jnp.float32
                )
            ).astype(jnp.bfloat16)
        gram = (
            domain_total(jnp.einsum("ca,cb->ab", block, block, preferred_element_type=jnp.float32))
            / cells
        )
        factor = jnp.linalg.cholesky(gram)
        inverse = jax.scipy.linalg.solve_triangular(factor, identity, lower=True)
        whitening = inverse.T.astype(jnp.bfloat16)
        pieces.append(
            jnp.dot(block, whitening, preferred_element_type=jnp.float32).astype(jnp.bfloat16)
        )
    return jnp.concatenate(pieces, axis=1).reshape(planes, NY, NX, bands)


def solution(mesh):
    return jax.shard_map(
        shards,
        mesh=mesh,
        in_specs=(P(("groups", "gz"), None, None, None), P(("groups", "gz"), None), P("groups")),
        out_specs=P(("groups", "gz"), None, None, None),
        check_vma=False,
    )
```

profile of v0, /device:TPU:0, one launch (start us, length us, event | category | flops | bytes accessed | tf_op | source)
XLA Modules:
  0.0 492.9 jit_solution(13511593628192767567)
XLA Ops:
  6.5 2.8 fusion.114
  9.3 2.4 collective-permute-start
  11.8 1.3 collective-permute-start.1
  13.1 0.7 fusion.115
  16.2 2.0 collective-permute-done.1
  18.3 0.7 convert_multiply_fusion.3
  19.2 6.6 %fusion.11 = bf16[6,8,64,256]{3,2,1,0:T(8,128)(2,1)S(1)} fusion(f32[6,8,64,256]{3,2,1,0:T(8,128)S(1)} %slice.356, f32[12,8,64,256]{3,2,1,0:T(8,128)S(1)} %convert_multiply_fusion.3, f32[6,8,64]{2,1,0:T(8,128)S(1)} %mul.191), kind=kLoop, calls=%fused_computation.66 | loop fusion | flops 22806528 | bytes 23605248 | tf_op jit(solution)/shard_map/convert_element_type | solution.py:81
  26.0 15.7 %collective-permute-start.2 = (bf16[3,8,64,256]{3,2,1,0:T(8,128)(2,1)S(1)}, bf16[3,8,64,256]{3,2,1,0:T(8,128)(2,1)S(1)}, u32[]{:S(2)}, u32[]{:S(2)}) collective-permute-start(bf16[3,8,64,256]{3,2,1,0:T(8,128)(2,1)S(1)} %get-tuple-element.11), channel_id=1, source_target_pairs={{0,1},{1,2},{2,3},{3,4},{4,5},{5,6},{6,7},{7,8},{8,9},{9,10},{10,1... | collective-permute-start | bytes 2359304 | tf_op jit(solution)/shard_map/ppermute | solution.py:21
  41.7 1.3 collective-permute-start.3
  43.0 0.5 collective-permute-done.2
  43.5 4.2 collective-permute-done.3
  47.7 0.7 convert_multiply_fusion.2
  48.5 2.0 slice.365
  50.5 18.8 %fusion.95 = bf16[6,8,64,256]{3,2,1,0:T(8,128)(2,1)S(1)} fusion(bf16[6,8,64,256]{3,2,1,0:T(8,128)(2,1)S(1)} %copy-done, f32[6,8,64,256]{3,2,1,0:T(8,128)} %slice.365, f32[12,8,64,256]{3,2,1,0:T(8,128)S(1)} %convert_multiply_fusion.2, f32[6,8,64]{2,1,0:T(8,128)S(1)} %mul.191), kind=kLoop, calls=%fused_computation.162 | loop fusion | flops 24379392 | bytes 25178112 | tf_op jit(solution)/shard_map/convert_element_type | solution.py:87
  69.5 15.6 %collective-permute-start.4 = (bf16[3,8,64,256]{3,2,1,0:T(8,128)(2,1)S(1)}, bf16[3,8,64,256]{3,2,1,0:T(8,128)(2,1)S(1)}, u32[]{:S(2)}, u32[]{:S(2)}) collective-permute-start(bf16[3,8,64,256]{3,2,1,0:T(8,128)(2,1)S(1)} %get-tuple-element.9), channel_id=1, source_target_pairs={{0,1},{1,2},{2,3},{3,4},{4,5},{5,6},{6,7},{7,8},{8,9},{9,10},{10,1... | collective-permute-start | bytes 2359304 | tf_op jit(solution)/shard_map/ppermute | solution.py:21
  85.1 1.3 collective-permute-start.5
  86.4 0.5 collective-permute-done.4
  87.0 4.3 collective-permute-done.5
  91.2 0.7 convert_multiply_fusion.1
  92.0 2.0 slice.374
  94.0 18.8 %fusion.94 = bf16[6,8,64,256]{3,2,1,0:T(8,128)(2,1)S(1)} fusion(bf16[6,8,64,256]{3,2,1,0:T(8,128)(2,1)S(1)} %fusion.11, f32[6,8,64,256]{3,2,1,0:T(8,128)} %slice.374, f32[12,8,64,256]{3,2,1,0:T(8,128)S(1)} %convert_multiply_fusion.1, f32[6,8,64]{2,1,0:T(8,128)S(1)} %mul.191), kind=kLoop, calls=%fused_computation.161 | loop fusion | flops 24379392 | bytes 25178112 | tf_op jit(solution)/shard_map/convert_element_type | solution.py:87
  113.0 15.6 %collective-permute-start.6 = (bf16[3,8,64,256]{3,2,1,0:T(8,128)(2,1)S(1)}, bf16[3,8,64,256]{3,2,1,0:T(8,128)(2,1)S(1)}, u32[]{:S(2)}, u32[]{:S(2)}) collective-permute-start(bf16[3,8,64,256]{3,2,1,0:T(8,128)(2,1)S(1)} %get-tuple-element.6), channel_id=1, source_target_pairs={{0,1},{1,2},{2,3},{3,4},{4,5},{5,6},{6,7},{7,8},{8,9},{9,10},{10,1... | collective-permute-start | bytes 2359304 | tf_op jit(solution)/shard_map/ppermute | solution.py:21
  128.7 1.3 collective-permute-start.7
  130.0 0.5 compare_convert_fusion.1
  130.5 4.3 collective-permute-done.7
  134.8 0.7 convert_multiply_fusion
  135.9 6.8 %fusion.93 = bf16[6,8,64,256]{3,2,1,0:T(8,128)(2,1)S(1)} fusion(bf16[6,8,64,256]{3,2,1,0:T(8,128)(2,1)S(1)} %fusion.95, f32[6,8,64,256]{3,2,1,0:T(8,128)S(1)} %slice.383, f32[12,8,64,256]{3,2,1,0:T(8,128)S(1)} %convert_multiply_fusion, f32[6,8,64]{2,1,0:T(8,128)S(1)} %mul.191), kind=kLoop, calls=%fused_computation.160 | loop fusion | flops 24379392 | bytes 25178112 | tf_op jit(solution)/shard_map/convert_element_type | solution.py:87
  143.0 0.9 broadcast_multiply_fusion.2
  144.2 1.2 fusion.110
  146.1 101.4 %all-reduce.12.cloned.1.call-done = f32[8,128,128]{2,1,0:T(8,128)} async-done(((f32[8,128,128]{2,1,0:T(8,128)}), f32[8,128,128]{2,1,0:T(8,128)}) %all-reduce.12.cloned.1.call-update) | async-done | bytes 524304 | tf_op jit(solution)/shard_map/psum | solution.py:94
  247.5 1.1 multiply_reduce_fusion.2
  248.9 11.7 %cholesky.44 = f32[128,128]{1,0:T(8,128)S(1)} custom-call(f32[128,128]{1,0:T(8,128)S(1)} %fusion.108), custom_call_target="Cholesky" | custom-call | tf_op jit(solution)/shard_map/jit(cholesky)/cholesky | solution.py:119
  260.6 0.6 compare_reduce_fusion.1
  261.3 0.7 fusion.103
  262.0 9.8 %custom-call.6 = f32[1,128,128]{1,2,0:T(8,128)S(1)} custom-call(f32[1,128,128]{2,1,0:T(8,128)S(1)} %fusion.103), custom_call_target="InvertDiagBlocksLowerTriangular" | custom-call | tf_op jit(solution)/shard_map/jit(_solve_triangular)/triangular_solve | solution.py:120
  272.8 0.9 broadcast_multiply_fusion.1
  274.0 91.0 %all-reduce.14.cloned.1.call-done = f32[8,128,128]{2,1,0:T(8,128)} async-done(((f32[8,128,128]{2,1,0:T(8,128)}), f32[8,128,128]{2,1,0:T(8,128)}) %all-reduce.14.cloned.1.call-update) | async-done | bytes 524304 | tf_op jit(solution)/shard_map/psum | solution.py:94
  365.0 1.1 multiply_reduce_fusion.1
  366.3 0.4 fusion
  366.7 0.4 fusion.116
  367.1 0.9 broadcast_multiply_fusion
  368.0 91.8 %all-reduce.16.cloned.1.call-done = f32[8,128,128]{2,1,0:T(8,128)} async-done(((f32[8,128,128]{2,1,0:T(8,128)}), f32[8,128,128]{2,1,0:T(8,128)}) %all-reduce.16.cloned.1.call-update) | async-done | bytes 524304 | tf_op jit(solution)/shard_map/psum | solution.py:94
  459.8 1.1 multiply_reduce_fusion
  461.2 11.7 %cholesky.55 = f32[128,128]{1,0:T(8,128)S(1)} custom-call(f32[128,128]{1,0:T(8,128)S(1)} %fusion.106), custom_call_target="Cholesky" | custom-call | tf_op jit(solution)/shard_map/jit(cholesky)/cholesky | solution.py:119
  472.9 0.6 compare_reduce_fusion
  473.6 0.7 fusion.104
  474.2 9.8 %custom-call.7 = f32[1,128,128]{1,2,0:T(8,128)S(1)} custom-call(f32[1,128,128]{2,1,0:T(8,128)S(1)} %fusion.104), custom_call_target="InvertDiagBlocksLowerTriangular" | custom-call | tf_op jit(solution)/shard_map/jit(_solve_triangular)/triangular_solve | solution.py:120
  484.8 1.6 copy.15
  (42 shorter events, 4.5 us)
Async XLA Ops:
  6.5 11.7 %copy-start = (bf16[6,8,64,256]{3,2,1,0:T(8,128)(2,1)S(1)}, bf16[6,8,64,256]{3,2,1,0:T(8,128)(2,1)}, u32[]{:S(2)}) copy-start(bf16[6,8,64,256]{3,2,1,0:T(8,128)(2,1)} %param.6) | copy-start | bytes 4718596
  6.5 6.6 %copy-start.2 = (s32[16]{0:T(128)S(1)}, s32[16]{0:T(128)}, u32[]{:S(2)}) copy-start(s32[16]{0:T(128)} %param.8) | copy-start | bytes 196
  6.5 9.5 %copy-start.1 = (f32[6,512]{1,0:T(8,128)S(1)}, f32[6,512]{1,0:T(8,128)}, u32[]{:S(2)}) copy-start(f32[6,512]{1,0:T(8,128)} %param.7) | copy-start | bytes 36868
  6.5 241.0 %all-reduce.12.cloned.1.call-start = ((), (), s32[]{:S(2)}) async-start(), calls=%async_computation | async-start | bytes 1048576 | tf_op jit(solution)/shard_map/psum | solution.py:94
  9.3 6.9 %collective-permute-start = (bf16[3,8,64,256]{3,2,1,0:T(8,128)(2,1)}, bf16[3,8,64,256]{3,2,1,0:T(8,128)(2,1)S(1)}, u32[]{:S(2)}, u32[]{:S(2)}) collective-permute-start(bf16[3,8,64,256]{3,2,1,0:T(8,128)(2,1)} %get-tuple-element.13), channel_id=1, source_target_pairs={{0,1},{1,2},{2,3},{3,4},{4,5},{5,6},{6,7},{7,8},{8,9},{9,10},{10,1... | collective-permute-start | bytes 2359304 | tf_op jit(solution)/shard_map/ppermute | solution.py:21
  11.8 6.5 %collective-permute-start.1 = (bf16[3,8,64,256]{3,2,1,0:T(8,128)(2,1)}, bf16[3,8,64,256]{3,2,1,0:T(8,128)(2,1)S(1)}, u32[]{:S(2)}, u32[]{:S(2)}) collective-permute-start(bf16[3,8,64,256]{3,2,1,0:T(8,128)(2,1)} %get-tuple-element.14), channel_id=1, source_target_pairs={{1,0},{2,1},{3,2},{4,3},{5,4},{6,5},{7,6},{8,7},{9,8},{10,9},{11,1... | collective-permute-start | bytes 2359304 | tf_op jit(solution)/shard_map/ppermute | solution.py:24
  26.0 17.6 %collective-permute-start.2 = (bf16[3,8,64,256]{3,2,1,0:T(8,128)(2,1)S(1)}, bf16[3,8,64,256]{3,2,1,0:T(8,128)(2,1)S(1)}, u32[]{:S(2)}, u32[]{:S(2)}) collective-permute-start(bf16[3,8,64,256]{3,2,1,0:T(8,128)(2,1)S(1)} %get-tuple-element.11), channel_id=1, source_target_pairs={{0,1},{1,2},{2,3},{3,4},{4,5},{5,6},{6,7},{7,8},{8,9},{9,10},{10,1... | collective-permute-start | bytes 2359304 | tf_op jit(solution)/shard_map/ppermute | solution.py:21
  41.7 6.0 %collective-permute-start.3 = (bf16[3,8,64,256]{3,2,1,0:T(8,128)(2,1)S(1)}, bf16[3,8,64,256]{3,2,1,0:T(8,128)(2,1)S(1)}, u32[]{:S(2)}, u32[]{:S(2)}) collective-permute-start(bf16[3,8,64,256]{3,2,1,0:T(8,128)(2,1)S(1)} %get-tuple-element.12), channel_id=1, source_target_pairs={{1,0},{2,1},{3,2},{4,3},{5,4},{6,5},{7,6},{8,7},{9,8},{10,9},{11,1... | collective-permute-start | bytes 2359304 | tf_op jit(solution)/shard_map/ppermute | solution.py:24
  69.5 17.5 %collective-permute-start.4 = (bf16[3,8,64,256]{3,2,1,0:T(8,128)(2,1)S(1)}, bf16[3,8,64,256]{3,2,1,0:T(8,128)(2,1)S(1)}, u32[]{:S(2)}, u32[]{:S(2)}) collective-permute-start(bf16[3,8,64,256]{3,2,1,0:T(8,128)(2,1)S(1)} %get-tuple-element.9), channel_id=1, source_target_pairs={{0,1},{1,2},{2,3},{3,4},{4,5},{5,6},{6,7},{7,8},{8,9},{9,10},{10,1... | collective-permute-start | bytes 2359304 | tf_op jit(solution)/shard_map/ppermute | solution.py:21
  85.1 6.1 %collective-permute-start.5 = (bf16[3,8,64,256]{3,2,1,0:T(8,128)(2,1)S(1)}, bf16[3,8,64,256]{3,2,1,0:T(8,128)(2,1)S(1)}, u32[]{:S(2)}, u32[]{:S(2)}) collective-permute-start(bf16[3,8,64,256]{3,2,1,0:T(8,128)(2,1)S(1)} %get-tuple-element.10), channel_id=1, source_target_pairs={{1,0},{2,1},{3,2},{4,3},{5,4},{6,5},{7,6},{8,7},{9,8},{10,9},{11,1... | collective-permute-start | bytes 2359304 | tf_op jit(solution)/shard_map/ppermute | solution.py:24
  113.0 17.5 %collective-permute-start.6 = (bf16[3,8,64,256]{3,2,1,0:T(8,128)(2,1)S(1)}, bf16[3,8,64,256]{3,2,1,0:T(8,128)(2,1)S(1)}, u32[]{:S(2)}, u32[]{:S(2)}) collective-permute-start(bf16[3,8,64,256]{3,2,1,0:T(8,128)(2,1)S(1)} %get-tuple-element.6), channel_id=1, source_target_pairs={{0,1},{1,2},{2,3},{3,4},{4,5},{5,6},{6,7},{7,8},{8,9},{9,10},{10,1... | collective-permute-start | bytes 2359304 | tf_op jit(solution)/shard_map/ppermute | solution.py:21
  128.7 6.1 %collective-permute-start.7 = (bf16[3,8,64,256]{3,2,1,0:T(8,128)(2,1)S(1)}, bf16[3,8,64,256]{3,2,1,0:T(8,128)(2,1)S(1)}, u32[]{:S(2)}, u32[]{:S(2)}) collective-permute-start(bf16[3,8,64,256]{3,2,1,0:T(8,128)(2,1)S(1)} %get-tuple-element.8), channel_id=1, source_target_pairs={{1,0},{2,1},{3,2},{4,3},{5,4},{6,5},{7,6},{8,7},{9,8},{10,9},{11,1... | collective-permute-start | bytes 2359304 | tf_op jit(solution)/shard_map/ppermute | solution.py:24
  144.0 221.1 %all-reduce.14.cloned.1.call-start = ((), (), s32[]{:S(2)}) async-start(), calls=%async_computation.1 | async-start | bytes 1048576 | tf_op jit(solution)/shard_map/psum | solution.py:94
  273.7 186.1 %all-reduce.16.cloned.1.call-start = ((), (), s32[]{:S(2)}) async-start(), calls=%async_computation.2 | async-start | bytes 1048576 | tf_op jit(solution)/shard_map/psum | solution.py:94
Sparse Core Ops, SparseCore 0:
  144.1 103.3 all-reduce.11
  273.8 91.1 all-reduce.13
  368.4 91.3 all-reduce.15
where the time goes:
time: 493 us
  waiting for transfers between devices  300 us (61%)
  other arithmetic  108 us (22%)
  starting transfers between devices  55 us (11%)
  between operations  16.5 us (3%)
  local copies, waits for them, and re-layouts  10.7 us (2%)
    psum x3, waiting for transfers between devices, domain_total(): summed = lax.psum(picker[:, None, None] * term[None], 'gz')  284 us
    ppermute x4, starting transfers between devices, extended_2(): lax.ppermute(lax.slice_in_dim(block, block.shape[dim] - width, None, axis...  49.4 us
    convert_element_type x3, other arithmetic, shards(): newer = (2.0 / EWIDTH * (image - CSHIFT * extended[3:-3]) - older.astype(...  44.4 us
    another operation x6, other arithmetic, shards(): factor = jnp.linalg.cholesky(gram)  24.8 us
    another operation x4, other arithmetic, shards(): inverse = jax.scipy.linalg.solve_triangular(factor, identity, lower=True)  20.9 us
    ppermute x4, waiting for transfers between devices, extended_2(): lax.ppermute(lax.slice_in_dim(block, 0, width, axis=dim), axis, backward)  14.7 us
  transfers between devices with their start and end apart: 11, of which 9 were waited for; matrix products, arithmetic and copies ran while one was open for 1% of the time, Pallas kernels for 0%

commit v1 on v0

--- a/solution.py
+++ b/solution.py
@@ -91,7 +91,7 @@
 
     def domain_total(term):
         picker = (jnp.arange(DOMS) == owner).astype(jnp.float32)
-        summed = lax.psum(picker[:, None, None] * term[None], "gz")
+        summed = jnp.sum(lax.all_gather(picker[:, None, None] * term[None], "gz"), axis=0)
         return jnp.sum(picker[:, None, None] * summed, axis=0)
 
     identity = jnp.eye(PANEL, dtype=jnp.float32)

time: 493 us -> 449 us (0.911)
  waiting for transfers between devices: 300 us -> 247 us
  other arithmetic: 108 us -> 116 us
    psum x3 -> x0, waiting for transfers between devices: 284 us -> none  [domain_total(): summed = lax.psum(picker[:, None, None] * term[None], 'gz')]
    all_gather x0 -> x3, waiting for transfers between devices: none -> 231 us  [domain_total(): lax.all_gather(picker[:, None, None] * term[None], 'gz')]
    reduce_sum x0 -> x3, other arithmetic: none -> 11.8 us  [domain_total(): jnp.sum(lax.all_gather(picker[:, None, None] * term[None], 'gz'), axis=0)]
where the time goes in v1:
time: 449 us; the launch traced here: 448 us
  waiting for transfers between devices  247 us (55%)
  other arithmetic  116 us (26%)
  starting transfers between devices  55 us (12%)
  between operations  16.5 us (4%)
  local copies, waits for them, and re-layouts  10.7 us (2%)
    all_gather x3, waiting for transfers between devices, domain_total(): lax.all_gather(picker[:, None, None] * term[None], 'gz')  231 us
    ppermute x4, starting transfers between devices, extended_2(): lax.ppermute(lax.slice_in_dim(block, block.shape[dim] - width, None, axis...  49.4 us
    convert_element_type x3, other arithmetic, shards(): newer = (2.0 / EWIDTH * (image - CSHIFT * extended[3:-3]) - older.astype(...  44.4 us
    another operation x6, other arithmetic, shards(): factor = jnp.linalg.cholesky(gram)  24.8 us
    another operation x4, other arithmetic, shards(): inverse = jax.scipy.linalg.solve_triangular(factor, identity, lower=True)  20.9 us
    ppermute x4, waiting for transfers between devices, extended_2(): lax.ppermute(lax.slice_in_dim(block, 0, width, axis=dim), axis, backward)  14.6 us
    reduce_sum x3, other arithmetic, domain_total(): jnp.sum(lax.all_gather(picker[:, None, None] * term[None], 'gz'), axis=0)  11.8 us
  transfers between devices with their start and end apart: 11, of which 9 were waited for; matrix products, arithmetic and copies ran while one was open for 1% of the time, Pallas kernels for 0%

profile of v1, /device:TPU:0, one launch (start us, length us, event | category | flops | bytes accessed | tf_op | source)
XLA Modules:
  0.0 448.2 jit_solution(7298900746538987689)
XLA Ops:
  6.5 2.8 fusion.114
  9.3 2.4 collective-permute-start
  11.8 1.3 collective-permute-start.1
  13.1 0.7 fusion.115
  16.3 2.0 collective-permute-done.1
  18.3 0.7 convert_multiply_fusion.3
  19.2 6.6 %fusion.11 = bf16[6,8,64,256]{3,2,1,0:T(8,128)(2,1)S(1)} fusion(f32[6,8,64,256]{3,2,1,0:T(8,128)S(1)} %slice.356, f32[12,8,64,256]{3,2,1,0:T(8,128)S(1)} %convert_multiply_fusion.3, f32[6,8,64]{2,1,0:T(8,128)S(1)} %mul.214), kind=kLoop, calls=%fused_computation.66 | loop fusion | flops 22806528 | bytes 23605248 | tf_op jit(solution)/shard_map/convert_element_type | solution.py:81
  26.0 15.7 %collective-permute-start.2 = (bf16[3,8,64,256]{3,2,1,0:T(8,128)(2,1)S(1)}, bf16[3,8,64,256]{3,2,1,0:T(8,128)(2,1)S(1)}, u32[]{:S(2)}, u32[]{:S(2)}) collective-permute-start(bf16[3,8,64,256]{3,2,1,0:T(8,128)(2,1)S(1)} %get-tuple-element.11), channel_id=1, source_target_pairs={{0,1},{1,2},{2,3},{3,4},{4,5},{5,6},{6,7},{7,8},{8,9},{9,10},{10,1... | collective-permute-start | bytes 2359304 | tf_op jit(solution)/shard_map/ppermute | solution.py:21
  41.7 1.3 collective-permute-start.3
  43.0 0.5 collective-permute-done.2
  43.5 4.2 collective-permute-done.3
  47.7 0.7 convert_multiply_fusion.2
  48.5 2.0 slice.365
  50.5 18.8 %fusion.95 = bf16[6,8,64,256]{3,2,1,0:T(8,128)(2,1)S(1)} fusion(bf16[6,8,64,256]{3,2,1,0:T(8,128)(2,1)S(1)} %copy-done, f32[6,8,64,256]{3,2,1,0:T(8,128)} %slice.365, f32[12,8,64,256]{3,2,1,0:T(8,128)S(1)} %convert_multiply_fusion.2, f32[6,8,64]{2,1,0:T(8,128)S(1)} %mul.214), kind=kLoop, calls=%fused_computation.162 | loop fusion | flops 24379392 | bytes 25178112 | tf_op jit(solution)/shard_map/convert_element_type | solution.py:87
  69.5 15.6 %collective-permute-start.4 = (bf16[3,8,64,256]{3,2,1,0:T(8,128)(2,1)S(1)}, bf16[3,8,64,256]{3,2,1,0:T(8,128)(2,1)S(1)}, u32[]{:S(2)}, u32[]{:S(2)}) collective-permute-start(bf16[3,8,64,256]{3,2,1,0:T(8,128)(2,1)S(1)} %get-tuple-element.9), channel_id=1, source_target_pairs={{0,1},{1,2},{2,3},{3,4},{4,5},{5,6},{6,7},{7,8},{8,9},{9,10},{10,1... | collective-permute-start | bytes 2359304 | tf_op jit(solution)/shard_map/ppermute | solution.py:21
  85.1 1.3 collective-permute-start.5
  86.4 0.5 collective-permute-done.4
  87.0 4.3 collective-permute-done.5
  91.2 0.7 convert_multiply_fusion.1
  92.0 2.0 slice.374
  94.0 18.8 %fusion.94 = bf16[6,8,64,256]{3,2,1,0:T(8,128)(2,1)S(1)} fusion(bf16[6,8,64,256]{3,2,1,0:T(8,128)(2,1)S(1)} %fusion.11, f32[6,8,64,256]{3,2,1,0:T(8,128)} %slice.374, f32[12,8,64,256]{3,2,1,0:T(8,128)S(1)} %convert_multiply_fusion.1, f32[6,8,64]{2,1,0:T(8,128)S(1)} %mul.214), kind=kLoop, calls=%fused_computation.161 | loop fusion | flops 24379392 | bytes 25178112 | tf_op jit(solution)/shard_map/convert_element_type | solution.py:87
  113.0 15.6 %collective-permute-start.6 = (bf16[3,8,64,256]{3,2,1,0:T(8,128)(2,1)S(1)}, bf16[3,8,64,256]{3,2,1,0:T(8,128)(2,1)S(1)}, u32[]{:S(2)}, u32[]{:S(2)}) collective-permute-start(bf16[3,8,64,256]{3,2,1,0:T(8,128)(2,1)S(1)} %get-tuple-element.6), channel_id=1, source_target_pairs={{0,1},{1,2},{2,3},{3,4},{4,5},{5,6},{6,7},{7,8},{8,9},{9,10},{10,1... | collective-permute-start | bytes 2359304 | tf_op jit(solution)/shard_map/ppermute | solution.py:21
  128.7 1.3 collective-permute-start.7
  130.0 0.6 compare_convert_fusion.1
  130.5 4.2 collective-permute-done.7
  134.8 0.7 convert_multiply_fusion
  135.9 6.8 %fusion.93 = bf16[6,8,64,256]{3,2,1,0:T(8,128)(2,1)S(1)} fusion(bf16[6,8,64,256]{3,2,1,0:T(8,128)(2,1)S(1)} %fusion.95, f32[6,8,64,256]{3,2,1,0:T(8,128)S(1)} %slice.383, f32[12,8,64,256]{3,2,1,0:T(8,128)S(1)} %convert_multiply_fusion, f32[6,8,64]{2,1,0:T(8,128)S(1)} %mul.214), kind=kLoop, calls=%fused_computation.160 | loop fusion | flops 24379392 | bytes 25178112 | tf_op jit(solution)/shard_map/convert_element_type | solution.py:87
  143.0 0.9 broadcast_multiply_fusion.2
  144.2 1.2 fusion.110
  146.0 85.1 %all-gather.4.cloned.1.call-done = f32[16,8,128,128]{3,2,1,0:T(8,128)} async-done(((f32[1,8,128,128]{3,2,1,0:T(8,128)}), f32[16,8,128,128]{3,2,1,0:T(8,128)}) %all-gather.4.cloned.1.call-update) | async-done | bytes 8388624 | tf_op jit(solution)/shard_map/all_gather | solution.py:94
  231.1 3.9 reduce_sum.63
  235.4 11.7 %cholesky.44 = f32[128,128]{1,0:T(8,128)S(1)} custom-call(f32[128,128]{1,0:T(8,128)S(1)} %fusion.108), custom_call_target="Cholesky" | custom-call | tf_op jit(solution)/shard_map/jit(cholesky)/cholesky | solution.py:119
  247.2 0.6 compare_reduce_fusion.1
  247.8 0.7 fusion.103
  248.5 9.8 %custom-call.6 = f32[1,128,128]{1,2,0:T(8,128)S(1)} custom-call(f32[1,128,128]{2,1,0:T(8,128)S(1)} %fusion.103), custom_call_target="InvertDiagBlocksLowerTriangular" | custom-call | tf_op jit(solution)/shard_map/jit(_solve_triangular)/triangular_solve | solution.py:120
  259.3 0.9 broadcast_multiply_fusion.1
  260.5 72.8 %all-gather.6.cloned.1.call-done = f32[16,8,128,128]{3,2,1,0:T(8,128)} async-done(((f32[1,8,128,128]{3,2,1,0:T(8,128)}), f32[16,8,128,128]{3,2,1,0:T(8,128)}) %all-gather.6.cloned.1.call-update) | async-done | bytes 8388624 | tf_op jit(solution)/shard_map/all_gather | solution.py:94
  333.3 3.9 reduce_sum.66
  337.4 0.4 fusion
  337.8 0.4 fusion.116
  338.3 0.9 broadcast_multiply_fusion
  339.2 73.0 %all-gather.8.cloned.1.call-done = f32[16,8,128,128]{3,2,1,0:T(8,128)} async-done(((f32[1,8,128,128]{3,2,1,0:T(8,128)}), f32[16,8,128,128]{3,2,1,0:T(8,128)}) %all-gather.8.cloned.1.call-update) | async-done | bytes 8388624 | tf_op jit(solution)/shard_map/all_gather | solution.py:94
  412.2 3.9 reduce_sum.68
  416.5 11.7 %cholesky.55 = f32[128,128]{1,0:T(8,128)S(1)} custom-call(f32[128,128]{1,0:T(8,128)S(1)} %fusion.106), custom_call_target="Cholesky" | custom-call | tf_op jit(solution)/shard_map/jit(cholesky)/cholesky | solution.py:119
  428.2 0.6 compare_reduce_fusion
  428.9 0.7 fusion.104
  429.5 9.8 %custom-call.7 = f32[1,128,128]{1,2,0:T(8,128)S(1)} custom-call(f32[1,128,128]{2,1,0:T(8,128)S(1)} %fusion.104), custom_call_target="InvertDiagBlocksLowerTriangular" | custom-call | tf_op jit(solution)/shard_map/jit(_solve_triangular)/triangular_solve | solution.py:120
  440.1 1.6 copy.18
  (45 shorter events, 4.8 us)
Async XLA Ops:
  6.5 11.7 %copy-start = (bf16[6,8,64,256]{3,2,1,0:T(8,128)(2,1)S(1)}, bf16[6,8,64,256]{3,2,1,0:T(8,128)(2,1)}, u32[]{:S(2)}) copy-start(bf16[6,8,64,256]{3,2,1,0:T(8,128)(2,1)} %param.6) | copy-start | bytes 4718596
  6.5 6.6 %copy-start.2 = (s32[16]{0:T(128)S(1)}, s32[16]{0:T(128)}, u32[]{:S(2)}) copy-start(s32[16]{0:T(128)} %param.8) | copy-start | bytes 196
  6.5 9.6 %copy-start.1 = (f32[6,512]{1,0:T(8,128)S(1)}, f32[6,512]{1,0:T(8,128)}, u32[]{:S(2)}) copy-start(f32[6,512]{1,0:T(8,128)} %param.7) | copy-start | bytes 36868
  6.5 224.6 %all-gather.4.cloned.1.call-start = ((), (), s32[]{:S(2)}) async-start(), calls=%async_computation | async-start | bytes 8912896 | tf_op jit(solution)/shard_map/all_gather | solution.py:94
  9.3 6.9 %collective-permute-start = (bf16[3,8,64,256]{3,2,1,0:T(8,128)(2,1)}, bf16[3,8,64,256]{3,2,1,0:T(8,128)(2,1)S(1)}, u32[]{:S(2)}, u32[]{:S(2)}) collective-permute-start(bf16[3,8,64,256]{3,2,1,0:T(8,128)(2,1)} %get-tuple-element.13), channel_id=1, source_target_pairs={{0,1},{1,2},{2,3},{3,4},{4,5},{5,6},{6,7},{7,8},{8,9},{9,10},{10,1... | collective-permute-start | bytes 2359304 | tf_op jit(solution)/shard_map/ppermute | solution.py:21
  11.8 6.5 %collective-permute-start.1 = (bf16[3,8,64,256]{3,2,1,0:T(8,128)(2,1)}, bf16[3,8,64,256]{3,2,1,0:T(8,128)(2,1)S(1)}, u32[]{:S(2)}, u32[]{:S(2)}) collective-permute-start(bf16[3,8,64,256]{3,2,1,0:T(8,128)(2,1)} %get-tuple-element.14), channel_id=1, source_target_pairs={{1,0},{2,1},{3,2},{4,3},{5,4},{6,5},{7,6},{8,7},{9,8},{10,9},{11,1... | collective-permute-start | bytes 2359304 | tf_op jit(solution)/shard_map/ppermute | solution.py:24
  26.0 17.6 %collective-permute-start.2 = (bf16[3,8,64,256]{3,2,1,0:T(8,128)(2,1)S(1)}, bf16[3,8,64,256]{3,2,1,0:T(8,128)(2,1)S(1)}, u32[]{:S(2)}, u32[]{:S(2)}) collective-permute-start(bf16[3,8,64,256]{3,2,1,0:T(8,128)(2,1)S(1)} %get-tuple-element.11), channel_id=1, source_target_pairs={{0,1},{1,2},{2,3},{3,4},{4,5},{5,6},{6,7},{7,8},{8,9},{9,10},{10,1... | collective-permute-start | bytes 2359304 | tf_op jit(solution)/shard_map/ppermute | solution.py:21
  41.7 6.0 %collective-permute-start.3 = (bf16[3,8,64,256]{3,2,1,0:T(8,128)(2,1)S(1)}, bf16[3,8,64,256]{3,2,1,0:T(8,128)(2,1)S(1)}, u32[]{:S(2)}, u32[]{:S(2)}) collective-permute-start(bf16[3,8,64,256]{3,2,1,0:T(8,128)(2,1)S(1)} %get-tuple-element.12), channel_id=1, source_target_pairs={{1,0},{2,1},{3,2},{4,3},{5,4},{6,5},{7,6},{8,7},{9,8},{10,9},{11,1... | collective-permute-start | bytes 2359304 | tf_op jit(solution)/shard_map/ppermute | solution.py:24
  69.5 17.5 %collective-permute-start.4 = (bf16[3,8,64,256]{3,2,1,0:T(8,128)(2,1)S(1)}, bf16[3,8,64,256]{3,2,1,0:T(8,128)(2,1)S(1)}, u32[]{:S(2)}, u32[]{:S(2)}) collective-permute-start(bf16[3,8,64,256]{3,2,1,0:T(8,128)(2,1)S(1)} %get-tuple-element.9), channel_id=1, source_target_pairs={{0,1},{1,2},{2,3},{3,4},{4,5},{5,6},{6,7},{7,8},{8,9},{9,10},{10,1... | collective-permute-start | bytes 2359304 | tf_op jit(solution)/shard_map/ppermute | solution.py:21
  85.1 6.1 %collective-permute-start.5 = (bf16[3,8,64,256]{3,2,1,0:T(8,128)(2,1)S(1)}, bf16[3,8,64,256]{3,2,1,0:T(8,128)(2,1)S(1)}, u32[]{:S(2)}, u32[]{:S(2)}) collective-permute-start(bf16[3,8,64,256]{3,2,1,0:T(8,128)(2,1)S(1)} %get-tuple-element.10), channel_id=1, source_target_pairs={{1,0},{2,1},{3,2},{4,3},{5,4},{6,5},{7,6},{8,7},{9,8},{10,9},{11,1... | collective-permute-start | bytes 2359304 | tf_op jit(solution)/shard_map/ppermute | solution.py:24
  113.0 17.5 %collective-permute-start.6 = (bf16[3,8,64,256]{3,2,1,0:T(8,128)(2,1)S(1)}, bf16[3,8,64,256]{3,2,1,0:T(8,128)(2,1)S(1)}, u32[]{:S(2)}, u32[]{:S(2)}) collective-permute-start(bf16[3,8,64,256]{3,2,1,0:T(8,128)(2,1)S(1)} %get-tuple-element.6), channel_id=1, source_target_pairs={{0,1},{1,2},{2,3},{3,4},{4,5},{5,6},{6,7},{7,8},{8,9},{9,10},{10,1... | collective-permute-start | bytes 2359304 | tf_op jit(solution)/shard_map/ppermute | solution.py:21
  128.7 6.1 %collective-permute-start.7 = (bf16[3,8,64,256]{3,2,1,0:T(8,128)(2,1)S(1)}, bf16[3,8,64,256]{3,2,1,0:T(8,128)(2,1)S(1)}, u32[]{:S(2)}, u32[]{:S(2)}) collective-permute-start(bf16[3,8,64,256]{3,2,1,0:T(8,128)(2,1)S(1)} %get-tuple-element.8), channel_id=1, source_target_pairs={{1,0},{2,1},{3,2},{4,3},{5,4},{6,5},{7,6},{8,7},{9,8},{10,9},{11,1... | collective-permute-start | bytes 2359304 | tf_op jit(solution)/shard_map/ppermute | solution.py:24
  144.0 189.3 %all-gather.6.cloned.1.call-start = ((), (), s32[]{:S(2)}) async-start(), calls=%async_computation.1 | async-start | bytes 8912896 | tf_op jit(solution)/shard_map/all_gather | solution.py:94
  260.2 152.0 %all-gather.8.cloned.1.call-start = ((), (), s32[]{:S(2)}) async-start(), calls=%async_computation.2 | async-start | bytes 8912896 | tf_op jit(solution)/shard_map/all_gather | solution.py:94
Sparse Core Ops, SparseCore 0:
  144.1 87.0 all-gather.3
  260.4 72.8 all-gather.5
  339.3 72.8 all-gather.7
